TPU v7x, 512 devices: a whole 4x8x8 slice. The times are simulated.
512 devices in a mesh: grp: 32 (over x, y), tp: 16 (over z, core).
Axes of the slice: x: 4, y: 8, z: 8, core: 2. Of those that a mesh axis runs over, the one named last changes fastest.
Arguments:
- patches: bfloat16 [16384, 1664], P('grp'), may hold values from -6 to 6
- patch_image: int32 [16384], P('grp'), may hold values from 0 to 4095, as said below
- vis_gain: float32 [1664], replicated, may hold values from 0.25 to 1.75
- vis_bias: float32 [1664], replicated, may hold values from -3 to 3
- vis_qkv: bfloat16 [3, 1664, 1664], P(None, None, 'tp'), may hold values from -2 to 2
- vis_out: bfloat16 [1664, 1664], P('tp'), may hold values from -0.15625 to 0.15625
- merge_weight: bfloat16 [4, 1664, 1024], P(None, 'tp'), may hold values from -0.078125 to 0.078125
- positions: int32 [4096], P('grp'), may hold values from 0 to 12287, as said below
- text: bfloat16 [8192, 1024], P('grp'), may hold values from -6 to 6
- dec_gain: float32 [1024], replicated, may hold values from 0.25 to 1.75
- dec_bias: float32 [1024], replicated, may hold values from -3 to 3
- dec_qkv: bfloat16 [3, 1024, 1024], P(None, None, 'tp'), may hold values from -2 to 2
Outputs:
- dec_attn: bfloat16 [12288, 1024], P('grp', 'tp')
Inputs may be any that keep to these rules, and one draw needn't show every extreme that they name: `patch_image`: each aligned run of four patches belongs to one image. Groups 2j and 2j+1 are partners: the last image of group 2j continues as the first image of group 2j+1; no other image is shared between groups. All positions are distinct; each group's block of 384 positions holds exactly 128 of them; the 128 merged rows of one group put at most 8 positions into any one group's block.
All inputs are finite; a program needn't handle non-finite values.
Results may differ from a plain program's by a relative error of at most 0.025.
Values may be sent and summed in bfloat16 or wider, within the bound.
No kernel may reach another device: no remote copies, remote signals or barrier semaphores. Data moves between devices by JAX's collectives and lax.ppermute only.
A program may use at most 128 MiB of HBM per device.

v0:
```python
import jax
import jax.numpy as jnp
from jax import lax
from jax.sharding import PartitionSpec as P

HD = 104
DH = 64
layer_eps = 1e-05


def swapped(value, axis, stride):
    return lax.ppermute(value, axis, [(i, i ^ 1 << stride) for i in range(lax.axis_size(axis))])


def normalize(values, gain, bias):
    mean = jnp.mean(values, axis=-1, keepdims=True)
    centred = values - mean
    spread = jnp.mean(centred * centred, axis=-1, keepdims=True)
    return centred * lax.rsqrt(spread + layer_eps) * gain + bias


def body(
    patches,
    patch_image,
    vis_gain,
    vis_bias,
    vis_qkv,
    vis_out,
    merge_weight,
    positions,
    text,
    dec_gain,
    dec_bias,
    dec_qkv,
):
    rows = patches.shape[0]
    heads = vis_qkv.shape[2] // HD
    patches_f = patches.astype(jnp.float32)
    normed = normalize(patches_f, vis_gain, vis_bias).astype(jnp.bfloat16)
    proj = jnp.einsum("pd,sde->spe", normed, vis_qkv, preferred_element_type=jnp.float32).astype(
        jnp.bfloat16
    )
    query = proj[0].reshape(rows, heads, HD)
    partner_kv, partner_ids = swapped((proj[1:], patch_image), "grp", 0)
    both_kv = jnp.concatenate([proj[1:], partner_kv], axis=1)
    both_ids = jnp.concatenate([patch_image, partner_ids], axis=0)
    keys = both_kv[0].reshape(2 * rows, heads, HD)
    values = both_kv[1].reshape(2 * rows, heads, HD)
    scores = jnp.einsum("phe,khe->hpk", query, keys, preferred_element_type=jnp.float32) * HD ** (
        -0.5
    )
    same = patch_image[:, None] == both_ids[None, :]
    top = jnp.max(jnp.where(same, scores, -1e30), axis=2, keepdims=True)
    expo = jnp.where(same, jnp.exp(scores - top), 0.0)
    weights = (expo / jnp.sum(expo, axis=2, keepdims=True)).astype(jnp.bfloat16)
    attended = jnp.einsum(
        "hpk,khe->phe", weights, values, preferred_element_type=jnp.float32
    ).astype(jnp.bfloat16)
    attended = attended.reshape(rows, heads * HD)
    width = patches.shape[1] // lax.axis_size("tp")
    mixed = lax.psum_scatter(
        lax.dot_general(
            vis_out, attended, (((0,), (1,)), ((), ())), preferred_element_type=jnp.float32
        ).astype(jnp.bfloat16),
        "tp",
        scatter_dimension=0,
        tiled=True,
    ).astype(jnp.float32)
    own_cols = lax.dynamic_slice_in_dim(patches_f, lax.axis_index("tp") * width, width, 1)
    visual = (mixed + own_cols.T).astype(jnp.bfloat16)
    windows = visual.reshape(width, rows // 4, 4)
    partial_rows = jnp.einsum(
        "cmk,kce->me", windows, merge_weight, preferred_element_type=jnp.float32
    )
    groups = lax.axis_size("grp")
    here = lax.axis_index("grp")
    merged_count = rows // 4
    text_count = text.shape[0]
    tok = text_count + merged_count
    cap = merged_count // min(groups, 16)
    target = positions // tok
    member = (target[:, None] == jnp.arange(groups, dtype=jnp.int32)[None, :]).astype(jnp.int32)
    rank = jnp.sum(jnp.cumsum(member, axis=0) * member, axis=1) - 1
    slot = target * cap + rank
    select = slot[None, :] == jnp.arange(groups * cap, dtype=jnp.int32)[:, None]
    select_bf = select.astype(jnp.bfloat16)
    bucket_pos = jnp.sum(jnp.where(select, positions[None, :] + 1, 0), axis=1) - 1
    merged = lax.psum(partial_rows.astype(jnp.bfloat16), "tp")
    packed = jnp.dot(select_bf, merged, preferred_element_type=jnp.float32).astype(jnp.bfloat16)
    got_rows, got_pos = (
        lax.all_to_all(packed, "grp", split_axis=0, concat_axis=0, tiled=True),
        lax.all_to_all(bucket_pos, "grp", split_axis=0, concat_axis=0, tiled=True),
    )
    local_pos = got_pos - here * tok
    place = jnp.arange(tok, dtype=jnp.int32)
    landing = (local_pos[None, :] == place[:, None]) & (got_pos[None, :] >= 0)
    image_here = jnp.any(landing, axis=1).astype(jnp.int32)
    text_index = place - (jnp.cumsum(image_here) - image_here)
    text_pick = (image_here[:, None] == 0) & (
        text_index[:, None] == jnp.arange(text_count, dtype=jnp.int32)[None, :]
    )
    prompt = jnp.dot(landing.astype(jnp.bfloat16), got_rows, preferred_element_type=jnp.float32)
    prompt = prompt + jnp.dot(
        text_pick.astype(jnp.bfloat16), text, preferred_element_type=jnp.float32
    )
    dnorm = normalize(prompt, dec_gain, dec_bias).astype(jnp.bfloat16)
    dproj = jnp.einsum("td,sde->ste", dnorm, dec_qkv, preferred_element_type=jnp.float32).astype(
        jnp.bfloat16
    )
    dheads = dec_qkv.shape[2] // DH
    dquery = dproj[0].reshape(tok, dheads, DH)
    query_pos = here * tok + place
    best = jnp.full((dheads, tok), -1e30, jnp.float32)
    key_rows = lax.all_gather(dproj[1], "grp", axis=0, tiled=True).reshape(-1, dheads, DH)
    value_rows = lax.all_gather(dproj[2], "grp", axis=0, tiled=True).reshape(-1, dheads, DH)
    key_pos = jnp.arange(key_rows.shape[0], dtype=jnp.int32)
    score = jnp.einsum(
        "the,rhe->htr", dquery, key_rows, preferred_element_type=jnp.float32
    ) * DH ** (-0.5)
    allowed = key_pos[None, :] <= query_pos[:, None]
    new_best = jnp.maximum(best, jnp.max(jnp.where(allowed[None], score, -1e30), axis=2))
    expo_d = jnp.where(allowed[None], jnp.exp(score - new_best[:, :, None]), 0.0)
    total = jnp.sum(expo_d, axis=2)
    acc = jnp.einsum(
        "htr,rhe->hte", expo_d.astype(jnp.bfloat16), value_rows, preferred_element_type=jnp.float32
    )
    best, total, acc = (new_best, total, acc)
    result = acc / total[:, :, None]
    return result.transpose(1, 0, 2).reshape(tok, dheads * DH).astype(jnp.bfloat16)


def solution(mesh):
    in_specs = (
        P("grp", None),
        P("grp"),
        P(),
        P(),
        P(None, None, "tp"),
        P("tp", None),
        P(None, "tp", None),
        P("grp"),
        P("grp", None),
        P(),
        P(),
        P(None, None, "tp"),
    )
    out_specs = P("grp", "tp")
    return jax.shard_map(body, mesh=mesh, in_specs=in_specs, out_specs=out_specs, check_vma=False)
```

profile of v0, /device:TPU:8, one launch (start us, length us, event | category | flops | bytes accessed | tf_op | source)
XLA Modules:
  0.0 415.6 jit_solution(2915710087922539153)
XLA Ops:
  6.6 1.9 convert_reduce_fusion
  8.6 0.6 multiply_reduce_fusion
  9.2 1.0 fusion.6
  10.3 7.7 %collective-permute-start = (bf16[2,512,104]{1,2,0:T(8,128)(2,1)S(1)}, bf16[2,512,104]{1,2,0:T(8,128)(2,1)S(1)}, u32[]{:S(2)}, u32[]{:S(2)}) collective-permute-start(bf16[2,512,104]{1,2,0:T(8,128)(2,1)S(1)} %slice.38), channel_id=1, source_target_pairs={{0,16},{16,0},{32,48},{48,32},{64,80},{80,64},{96,112},{112,96},{1... | collective-permute-start | bytes 638984 | tf_op jit(solution)/shard_map/ppermute | solution.py:12
  18.1 1.9 collective-permute-start.1
  20.0 3.6 collective-permute-done.1
  23.6 0.6 fusion.5
  24.2 1.4 copy-done.2
  25.5 0.7 fusion.13
  26.2 4.3 %fusion.4 = bf16[1664,512]{0,1:T(8,128)(2,1)} fusion(bf16[104,1664]{1,0:T(8,128)(2,1)S(1)} %copy-done.6, f32[512,1024]{1,0:T(8,128)} %copy-done.2, f32[512]{0:T(512)S(1)} %fusion.13, f32[512]{0:T(512)S(1)} %get-tuple-element.11, s32[1024]{0:T(1024)S(1)} %pad_add_fusion, s32[512]{0:T(512)S(1)} %copy-done.4, bf16[2,512,104]{1,2,0:T(8,128)(2,1)S(1)} %slice.38, ...), kind=kOutput, calls=%fused_computation.10 | convolution fusion | flops 290738176 | bytes 4583424 | tf_op jit(solution)/shard_map/dot_general | solution.py:62
  30.5 3.6 copy.17
  34.2 2.0 convert_element_type.82
  36.8 59.7 %reduce-scatter.4.cloned.1.call-done = bf16[104,512]{1,0:T(8,128)(2,1)} async-done(((bf16[1664,512]{1,0:T(8,128)(2,1)}), bf16[104,512]{1,0:T(8,128)(2,1)}) %reduce-scatter.4.cloned.1.call-update) | async-done | bytes 106512
  96.5 1.0 copy.18
  97.5 1.2 fusion.49
  98.7 2.2 fusion.15
  100.9 0.7 sub.80
  101.6 9.9 %all-to-all-start = ((s32[32,8,1]{1,2,0:T(1,128)}), s32[32,8,1]{1,2,0:T(1,128)S(1)}, u32[]{:S(2)}, u32[]{:S(2)}) async-start(s32[32,8,1]{1,2,0:T(1,128)} %bitcast), calls=%async_computation | async-start | bytes 32768 | tf_op jit(solution)/shard_map/all_to_all | solution.py:92
  111.5 102.0 %all-reduce.2.cloned.1.call-done = bf16[128,1024]{1,0:T(8,128)(2,1)} async-done(((bf16[128,1024]{1,0:T(8,128)(2,1)}), bf16[128,1024]{1,0:T(8,128)(2,1)}) %all-reduce.2.cloned.1.call-update) | async-done | bytes 262160 | tf_op jit(solution)/shard_map/psum | solution.py:88
  213.5 2.0 fusion.14
  215.5 9.8 %all-to-all-start.1 = ((bf16[32,8,1024]{2,1,0:T(8,128)(2,1)}), bf16[32,8,1024]{2,1,0:T(8,128)(2,1)S(1)}, u32[]{:S(2)}, u32[]{:S(2)}) async-start(bf16[32,8,1024]{2,1,0:T(8,128)(2,1)} %fusion.14), calls=%async_computation.1 | async-start | bytes 1048576 | tf_op jit(solution)/shard_map/all_to_all | solution.py:91
  226.5 16.5 %all-to-all-done.1 = bf16[32,8,1024]{2,1,0:T(8,128)(2,1)S(1)} async-done(((bf16[32,8,1024]{2,1,0:T(8,128)(2,1)}), bf16[32,8,1024]{2,1,0:T(8,128)(2,1)S(1)}, u32[]{:S(2)}, u32[]{:S(2)}) %all-to-all-start.1) | async-done | bytes 524320 | tf_op jit(solution)/shard_map/all_to_all | solution.py:91
  243.0 0.4 fusion.42
  243.4 0.5 fusion.75
  244.4 0.5 fusion.37
  245.0 0.6 fusion.74
  245.9 0.3 all-gather.7.cloned.1.call-update
  246.3 71.2 %all-gather.5.cloned.1.call-done = bf16[1,12288,64]{1,2,0:T(8,128)(2,1)} async-done(((bf16[1,384,64]{1,2,0:T(8,128)(2,1)}), bf16[1,12288,64]{1,2,0:T(8,128)(2,1)}) %all-gather.5.cloned.1.call-update) | async-done | bytes 1572880 | tf_op jit(solution)/shard_map/all_gather | solution.py:114
  317.4 9.3 %select_reduce_fusion = (f32[384]{0:T(512)S(1)}, f32[384,12288]{1,0:T(8,128)}) fusion(s32[384]{0:T(512)S(1)} %iota_add_fusion, bf16[1,12288,64]{1,2,0:T(8,128)(2,1)} %all-gather.5.cloned.1.call-done, bf16[3,384,64]{1,2,0:T(8,128)(2,1)S(1)} %convert_bitcast_fusion.1), kind=kOutput, calls=%fused_computation.1 | convolution fusion | flops 622853760 | bytes 20499968 | tf_op jit(solution)/shard_map/the,rhe->htr/dot_general | solution.py:117
  326.7 11.1 %fusion = f32[384]{0:T(512)S(1)} fusion(f32[384,12288]{1,0:T(8,128)} %get-tuple-element.16, f32[384]{0:T(512)S(1)} %broadcast_maximum_fusion, s32[384]{0:T(512)S(1)} %iota_add_fusion), kind=kLoop, calls=%fused_computation.4 | loop fusion | flops 18873984 | bytes 18878976 | tf_op jit(solution)/shard_map/reduce_sum | solution.py:123
  337.8 60.2 %all-gather.7.cloned.1.call-done = bf16[1,12288,64]{1,2,0:T(8,128)(2,1)} async-done(((bf16[1,384,64]{1,2,0:T(8,128)(2,1)}), bf16[1,12288,64]{1,2,0:T(8,128)(2,1)}) %all-gather.7.cloned.1.call-update) | async-done | bytes 1572880 | tf_op jit(solution)/shard_map/all_gather | solution.py:115
  398.0 11.1 %fusion.22 = bf16[384,64]{0,1:T(8,128)(2,1)} fusion(bf16[1,12288,64]{1,2,0:T(8,128)(2,1)} %all-gather.7.cloned.1.call-done, f32[384,12288]{1,0:T(8,128)} %get-tuple-element.16, f32[384]{0:T(512)S(1)} %broadcast_maximum_fusion, s32[384]{0:T(512)S(1)} %iota_add_fusion, f32[384]{0:T(512)S(1)} %fusion), kind=kOutput, calls=%fused_computation.34 | convolution fusion | flops 622903296 | bytes 20500992 | tf_op jit(solution)/shard_map/htr,rhe->hte/dot_general | solution.py:124
  (61 shorter events, 2.8 us)
Async XLA Ops:
  6.5 2.6 copy-start
  6.5 2.1 copy-start.1
  6.5 2.7 copy-start.8
  6.5 2.7 copy-start.7
  6.5 89.9 %reduce-scatter.4.cloned.1.call-start = ((), (), s32[]{:S(2)}) async-start(), calls=%async_computation.6 | async-start | bytes 1810432
  9.2 8.9 %copy-start.4 = (s32[512]{0:T(512)S(1)}, s32[512]{0:T(512)}, u32[]{:S(2)}) copy-start(s32[512]{0:T(512)} %param.13) | copy-start | bytes 6148
  10.3 13.2 %collective-permute-start = (bf16[2,512,104]{1,2,0:T(8,128)(2,1)S(1)}, bf16[2,512,104]{1,2,0:T(8,128)(2,1)S(1)}, u32[]{:S(2)}, u32[]{:S(2)}) collective-permute-start(bf16[2,512,104]{1,2,0:T(8,128)(2,1)S(1)} %slice.38), channel_id=1, source_target_pairs={{0,16},{16,0},{32,48},{48,32},{64,80},{80,64},{96,112},{112,96},{1... | collective-permute-start | bytes 638984 | tf_op jit(solution)/shard_map/ppermute | solution.py:12
  18.1 5.5 %collective-permute-start.1 = (s32[512]{0:T(512)S(1)}, s32[512]{0:T(512)S(1)}, u32[]{:S(2)}, u32[]{:S(2)}) collective-permute-start(s32[512]{0:T(512)S(1)} %copy-done.4), channel_id=1, source_target_pairs={{0,16},{16,0},{32,48},{48,32},{64,80},{80,64},{96,112},{112,96},{1... | collective-permute-start | bytes 6152 | tf_op jit(solution)/shard_map/ppermute | solution.py:12
  23.6 2.6 copy-start.6
  24.2 1.4 copy-start.2
  34.1 179.3 %all-reduce.2.cloned.1.call-start = ((), (), s32[]{:S(2)}) async-start(), calls=%async_computation.3 | async-start | bytes 524288 | tf_op jit(solution)/shard_map/psum | solution.py:88
  34.2 2.0 copy-start.11
  100.9 142.5 %copy-start.3 = (bf16[256,1024]{1,0:T(8,128)(2,1)S(1)}, bf16[256,1024]{1,0:T(8,128)(2,1)}, u32[]{:S(2)}) copy-start(bf16[256,1024]{1,0:T(8,128)(2,1)} %param.20) | copy-start | bytes 1572868
  101.6 113.9 %all-to-all-start = ((s32[32,8,1]{1,2,0:T(1,128)}), s32[32,8,1]{1,2,0:T(1,128)S(1)}, u32[]{:S(2)}, u32[]{:S(2)}) async-start(s32[32,8,1]{1,2,0:T(1,128)} %bitcast), calls=%async_computation | async-start | bytes 32768 | tf_op jit(solution)/shard_map/all_to_all | solution.py:92
  215.5 27.5 %all-to-all-start.1 = ((bf16[32,8,1024]{2,1,0:T(8,128)(2,1)}), bf16[32,8,1024]{2,1,0:T(8,128)(2,1)S(1)}, u32[]{:S(2)}, u32[]{:S(2)}) async-start(bf16[32,8,1024]{2,1,0:T(8,128)(2,1)} %fusion.14), calls=%async_computation.1 | async-start | bytes 1048576 | tf_op jit(solution)/shard_map/all_to_all | solution.py:91
  225.4 92.1 %all-gather.5.cloned.1.call-start = ((), (), s32[]{:S(2)}) async-start(), calls=%async_computation.4 | async-start | bytes 1622016 | tf_op jit(solution)/shard_map/all_gather | solution.py:114
  243.4 1.0 copy-start.5
  243.4 1.0 copy-start.9
  243.4 1.0 copy-start.10
  245.7 152.3 %all-gather.7.cloned.1.call-start = ((), (), s32[]{:S(2)}) async-start(), calls=%async_computation.5 | async-start | bytes 1622016 | tf_op jit(solution)/shard_map/all_gather | solution.py:115
Sparse Core Ops, SparseCore 0:
  34.3 62.1 reduce-scatter.3
  101.0 112.4 all-reduce.1
  245.8 71.5 all-gather.4
  320.4 77.5 all-gather.6
where the time goes:
time: 416 us
  waiting for transfers between devices  313 us (75%)
  matrix products  32 us (8%)
  starting transfers between devices  29.7 us (7%)
  other arithmetic  19 us (5%)
  between operations  13.4 us (3%)
  local copies, waits for them, and re-layouts  8.01 us (2%)
    psum x1, waiting for transfers between devices, body(): merged = lax.psum(partial_rows.astype(jnp.bfloat16), 'tp')  102 us
    all_gather x1, waiting for transfers between devices, body(): lax.all_gather(dproj[1], 'grp', axis=0, tiled=True).reshape(-1, dheads, DH)  71.2 us
    all_gather x1, waiting for transfers between devices, body(): lax.all_gather(dproj[2], 'grp', axis=0, tiled=True).reshape(-1, dheads, DH)  60.2 us
    unnamed x5, waiting for transfers between devices  60.1 us
    all_to_all x1, waiting for transfers between devices, body(): lax.all_to_all(packed, 'grp', split_axis=0, concat_axis=0, tiled=True)  16.5 us
    dot_general x1, matrix products, body(): jnp.einsum('htr,rhe->hte', expo_d.astype(jnp.bfloat16), value_rows, prefe...  11.1 us
    reduce_sum x1, other arithmetic, body(): total = jnp.sum(expo_d, axis=2)  11.1 us
    all_to_all x1, starting transfers between devices, body(): lax.all_to_all(bucket_pos, 'grp', split_axis=0, concat_axis=0, tiled=True)  9.88 us
  transfers between devices with their start and end apart: 8, of which 6 were waited for; matrix products, arithmetic and copies ran while one was open for 6% of the time, Pallas kernels for 0%

commit v1 on v0

--- a/solution.py
+++ b/solution.py
@@ -6,6 +6,11 @@
 HD = 104
 DH = 64
 layer_eps = 1e-05
+
+
+def all_by_exchange(block, axis, dim):
+    sent = jnp.stack([block] * lax.axis_size(axis))
+    return jnp.concatenate(lax.all_to_all(sent, axis, 0, 0), axis=dim)
 
 
 def swapped(value, axis, stride):
@@ -111,7 +116,7 @@
     dquery = dproj[0].reshape(tok, dheads, DH)
     query_pos = here * tok + place
     best = jnp.full((dheads, tok), -1e30, jnp.float32)
-    key_rows = lax.all_gather(dproj[1], "grp", axis=0, tiled=True).reshape(-1, dheads, DH)
+    key_rows = all_by_exchange(dproj[1], "grp", 0).reshape(-1, dheads, DH)
     value_rows = lax.all_gather(dproj[2], "grp", axis=0, tiled=True).reshape(-1, dheads, DH)
     key_pos = jnp.arange(key_rows.shape[0], dtype=jnp.int32)
     score = jnp.einsum(

time: 416 us -> 354 us (0.85)
  waiting for transfers between devices: 313 us -> 245 us
  starting transfers between devices: 29.7 us -> 34.5 us
    all_gather x1 -> x0, waiting for transfers between devices: 71.2 us -> none  [body(): lax.all_gather(dproj[1], 'grp', axis=0, tiled=True).reshape(-1, dheads, DH)]
    all_to_all x0 -> x1, waiting for transfers between devices: none -> 39 us  [all_by_exchange(): return jnp.concatenate(lax.all_to_all(sent, axis, 0, 0), axis=dim)]
    all_gather x1, waiting for transfers between devices: 60.2 us -> 24.1 us  [body(): lax.all_gather(dproj[2], 'grp', axis=0, tiled=True).reshape(-1, dheads, DH)]
    all_to_all x0 -> x1, starting transfers between devices: none -> 4.86 us  [all_by_exchange(): return jnp.concatenate(lax.all_to_all(sent, axis, 0, 0), axis=dim)]
    unnamed x5 -> x4, waiting for transfers between devices: 60.1 us -> 60.2 us
  transfers between devices with their start and end apart: 8 -> 8, of which waited for: 6 -> 6; matrix products, arithmetic and copies ran while one was open for 6% -> 7% of each run, Pallas kernels for 0% -> 0%
where the time goes in v1:
time: 354 us; the launch traced here: 353 us
  waiting for transfers between devices  245 us (69%)
  starting transfers between devices  34.5 us (10%)
  matrix products  31 us (9%)
  other arithmetic  19 us (5%)
  between operations  13.4 us (4%)
  local copies, waits for them, and re-layouts  9.56 us (3%)
    psum x1, waiting for transfers between devices, body(): merged = lax.psum(partial_rows.astype(jnp.bfloat16), 'tp')  102 us
    unnamed x4, waiting for transfers between devices  60.2 us
    all_to_all x1, waiting for transfers between devices, all_by_exchange(): return jnp.concatenate(lax.all_to_all(sent, axis, 0, 0), axis=dim)  39 us
    all_gather x1, waiting for transfers between devices, body(): lax.all_gather(dproj[2], 'grp', axis=0, tiled=True).reshape(-1, dheads, DH)  24.1 us
    all_to_all x1, waiting for transfers between devices, body(): lax.all_to_all(packed, 'grp', split_axis=0, concat_axis=0, tiled=True)  16.6 us
    dot_general x1, matrix products, body(): jnp.einsum('htr,rhe->hte', expo_d.astype(jnp.bfloat16), value_rows, prefe...  11.1 us
    reduce_sum x1, other arithmetic, body(): total = jnp.sum(expo_d, axis=2)  11.1 us
    all_to_all x1, starting transfers between devices, body(): lax.all_to_all(bucket_pos, 'grp', split_axis=0, concat_axis=0, tiled=True)  9.88 us
  transfers between devices with their start and end apart: 8, of which 6 were waited for; matrix products, arithmetic and copies ran while one was open for 7% of the time, Pallas kernels for 0%

profile of v1, /device:TPU:8, one launch (start us, length us, event | category | flops | bytes accessed | tf_op | source)
XLA Modules:
  0.0 352.9 jit_solution(12014397949162417747)
XLA Ops:
  6.6 1.9 convert_reduce_fusion
  8.6 0.6 multiply_reduce_fusion
  9.2 1.0 fusion.6
  10.3 7.7 %collective-permute-start = (bf16[2,512,104]{1,2,0:T(8,128)(2,1)S(1)}, bf16[2,512,104]{1,2,0:T(8,128)(2,1)S(1)}, u32[]{:S(2)}, u32[]{:S(2)}) collective-permute-start(bf16[2,512,104]{1,2,0:T(8,128)(2,1)S(1)} %slice.41), channel_id=1, source_target_pairs={{0,16},{16,0},{32,48},{48,32},{64,80},{80,64},{96,112},{112,96},{1... | collective-permute-start | bytes 638984 | tf_op jit(solution)/shard_map/ppermute | solution.py:17
  18.1 1.9 collective-permute-start.1
  20.0 3.6 %collective-permute-done.1 = s32[512]{0:T(512)S(1)} collective-permute-done((s32[512]{0:T(512)S(1)}, s32[512]{0:T(512)S(1)}, u32[]{:S(2)}, u32[]{:S(2)}) %collective-permute-start.1) | collective-permute-done | bytes 2080 | tf_op jit(solution)/shard_map/ppermute | solution.py:17
  23.6 0.6 fusion.5
  24.2 1.4 copy-done.2
  25.5 0.7 fusion.12
  26.2 4.3 %fusion.4 = bf16[1664,512]{0,1:T(8,128)(2,1)} fusion(bf16[104,1664]{1,0:T(8,128)(2,1)S(1)} %copy-done.6, f32[512,1024]{1,0:T(8,128)} %copy-done.2, f32[512]{0:T(512)S(1)} %fusion.12, f32[512]{0:T(512)S(1)} %get-tuple-element.11, s32[1024]{0:T(1024)S(1)} %pad_add_fusion, s32[512]{0:T(512)S(1)} %copy-done.4, bf16[2,512,104]{1,2,0:T(8,128)(2,1)S(1)} %slice.41, ...), kind=kOutput, calls=%fused_computation.10 | convolution fusion | flops 290738176 | bytes 4583424 | tf_op jit(solution)/shard_map/dot_general | solution.py:67
  30.5 3.6 %copy.23 = bf16[1664,512]{1,0:T(8,128)(2,1)} copy(bf16[1664,512]{0,1:T(8,128)(2,1)} %fusion.4) | data formatting | bytes 3407872
  34.2 2.0 convert_element_type.82
  36.8 59.7 %reduce-scatter.4.cloned.1.call-done = bf16[104,512]{1,0:T(8,128)(2,1)} async-done(((bf16[1664,512]{1,0:T(8,128)(2,1)}), bf16[104,512]{1,0:T(8,128)(2,1)}) %reduce-scatter.4.cloned.1.call-update) | async-done | bytes 106512
  96.5 1.0 copy.24
  97.5 1.2 fusion.48
  98.7 2.2 fusion.14
  100.9 0.7 sub.80
  101.6 9.9 %all-to-all-start = ((s32[32,8,1]{1,2,0:T(1,128)}), s32[32,8,1]{1,2,0:T(1,128)S(1)}, u32[]{:S(2)}, u32[]{:S(2)}) async-start(s32[32,8,1]{1,2,0:T(1,128)} %bitcast), calls=%async_computation | async-start | bytes 32768 | tf_op jit(solution)/shard_map/all_to_all | solution.py:97
  111.5 102.0 %all-reduce.2.cloned.1.call-done = bf16[128,1024]{1,0:T(8,128)(2,1)} async-done(((bf16[128,1024]{1,0:T(8,128)(2,1)}), bf16[128,1024]{1,0:T(8,128)(2,1)}) %all-reduce.2.cloned.1.call-update) | async-done | bytes 262160 | tf_op jit(solution)/shard_map/psum | solution.py:93
  213.5 2.0 fusion.13
  215.5 9.8 %all-to-all-start.1 = ((bf16[32,8,1024]{2,1,0:T(8,128)(2,1)}), bf16[32,8,1024]{2,1,0:T(8,128)(2,1)S(1)}, u32[]{:S(2)}, u32[]{:S(2)}) async-start(bf16[32,8,1024]{2,1,0:T(8,128)(2,1)} %fusion.13), calls=%async_computation.1 | async-start | bytes 1048576 | tf_op jit(solution)/shard_map/all_to_all | solution.py:96
  226.5 16.6 %all-to-all-done.1 = bf16[32,8,1024]{2,1,0:T(8,128)(2,1)S(1)} async-done(((bf16[32,8,1024]{2,1,0:T(8,128)(2,1)}), bf16[32,8,1024]{2,1,0:T(8,128)(2,1)S(1)}, u32[]{:S(2)}, u32[]{:S(2)}) %all-to-all-start.1) | async-done | bytes 524320 | tf_op jit(solution)/shard_map/all_to_all | solution.py:96
  243.4 0.5 fusion.73
  244.4 0.5 fusion.36
  245.0 0.6 slice_bitcast_fusion.2
  245.6 1.4 stack.3
  247.0 4.9 %all-to-all-start.2 = ((bf16[32,384,64]{1,2,0:T(8,128)(2,1)}), bf16[32,384,64]{1,2,0:T(8,128)(2,1)S(1)}, u32[]{:S(2)}, u32[]{:S(2)}) async-start(bf16[32,384,64]{1,2,0:T(8,128)(2,1)} %stack.3), calls=%async_computation.2 | async-start | bytes 3145728 | tf_op jit(solution)/shard_map/all_to_all | solution.py:13
  252.6 39.0 %all-to-all-done.2 = bf16[32,384,64]{1,2,0:T(8,128)(2,1)S(1)} async-done(((bf16[32,384,64]{1,2,0:T(8,128)(2,1)}), bf16[32,384,64]{1,2,0:T(8,128)(2,1)S(1)}, u32[]{:S(2)}, u32[]{:S(2)}) %all-to-all-start.2) | async-done | bytes 1572896 | tf_op jit(solution)/shard_map/all_to_all | solution.py:13
  291.9 8.3 %select_reduce_fusion = (f32[384]{0:T(512)S(1)}, f32[384,12288]{1,0:T(8,128)}) fusion(s32[384]{0:T(512)S(1)} %iota_add_fusion, bf16[12288,64]{0,1:T(8,128)(2,1)S(1)} %bitcast.81, bf16[3,384,64]{1,2,0:T(8,128)(2,1)S(1)} %convert_bitcast_fusion.1), kind=kOutput, calls=%fused_computation.1 | convolution fusion | flops 622853760 | bytes 20499968 | tf_op jit(solution)/shard_map/the,rhe->htr/dot_general | solution.py:122
  300.2 11.1 %fusion = f32[384]{0:T(512)S(1)} fusion(f32[384,12288]{1,0:T(8,128)} %get-tuple-element.16, f32[384]{0:T(512)S(1)} %broadcast_maximum_fusion, s32[384]{0:T(512)S(1)} %iota_add_fusion), kind=kLoop, calls=%fused_computation.4 | loop fusion | flops 18873984 | bytes 18878976 | tf_op jit(solution)/shard_map/reduce_sum | solution.py:128
  311.2 24.1 %all-gather.3.cloned.1.call-done = bf16[1,12288,64]{1,2,0:T(8,128)(2,1)} async-done(((bf16[1,384,64]{1,2,0:T(8,128)(2,1)}), bf16[1,12288,64]{1,2,0:T(8,128)(2,1)}) %all-gather.3.cloned.1.call-update) | async-done | bytes 1572880 | tf_op jit(solution)/shard_map/all_gather | solution.py:120
  335.3 11.1 %fusion.21 = bf16[384,64]{0,1:T(8,128)(2,1)} fusion(bf16[1,12288,64]{1,2,0:T(8,128)(2,1)} %all-gather.3.cloned.1.call-done, f32[384,12288]{1,0:T(8,128)} %get-tuple-element.16, f32[384]{0:T(512)S(1)} %broadcast_maximum_fusion, s32[384]{0:T(512)S(1)} %iota_add_fusion, f32[384]{0:T(512)S(1)} %fusion), kind=kOutput, calls=%fused_computation.33 | convolution fusion | flops 622903296 | bytes 20500992 | tf_op jit(solution)/shard_map/htr,rhe->hte/dot_general | solution.py:129
  (62 shorter events, 3.7 us)
Async XLA Ops:
  6.5 2.6 copy-start
  6.5 2.1 copy-start.1
  6.5 2.7 copy-start.8
  6.5 2.7 copy-start.7
  6.5 89.9 %reduce-scatter.4.cloned.1.call-start = ((), (), s32[]{:S(2)}) async-start(), calls=%async_computation.6 | async-start | bytes 1810432
  9.2 8.9 %copy-start.4 = (s32[512]{0:T(512)S(1)}, s32[512]{0:T(512)}, u32[]{:S(2)}) copy-start(s32[512]{0:T(512)} %param.13) | copy-start | bytes 6148
  10.3 13.2 %collective-permute-start = (bf16[2,512,104]{1,2,0:T(8,128)(2,1)S(1)}, bf16[2,512,104]{1,2,0:T(8,128)(2,1)S(1)}, u32[]{:S(2)}, u32[]{:S(2)}) collective-permute-start(bf16[2,512,104]{1,2,0:T(8,128)(2,1)S(1)} %slice.41), channel_id=1, source_target_pairs={{0,16},{16,0},{32,48},{48,32},{64,80},{80,64},{96,112},{112,96},{1... | collective-permute-start | bytes 638984 | tf_op jit(solution)/shard_map/ppermute | solution.py:17
  18.1 5.5 %collective-permute-start.1 = (s32[512]{0:T(512)S(1)}, s32[512]{0:T(512)S(1)}, u32[]{:S(2)}, u32[]{:S(2)}) collective-permute-start(s32[512]{0:T(512)S(1)} %copy-done.4), channel_id=1, source_target_pairs={{0,16},{16,0},{32,48},{48,32},{64,80},{80,64},{96,112},{112,96},{1... | collective-permute-start | bytes 6152 | tf_op jit(solution)/shard_map/ppermute | solution.py:17
  23.6 2.6 copy-start.6
  24.2 1.4 copy-start.2
  34.1 179.3 %all-reduce.2.cloned.1.call-start = ((), (), s32[]{:S(2)}) async-start(), calls=%async_computation.4 | async-start | bytes 524288 | tf_op jit(solution)/shard_map/psum | solution.py:93
  34.2 2.0 copy-start.11
  100.9 142.5 %copy-start.3 = (bf16[256,1024]{1,0:T(8,128)(2,1)S(1)}, bf16[256,1024]{1,0:T(8,128)(2,1)}, u32[]{:S(2)}) copy-start(bf16[256,1024]{1,0:T(8,128)(2,1)} %param.20) | copy-start | bytes 1572868
  101.6 113.9 %all-to-all-start = ((s32[32,8,1]{1,2,0:T(1,128)}), s32[32,8,1]{1,2,0:T(1,128)S(1)}, u32[]{:S(2)}, u32[]{:S(2)}) async-start(s32[32,8,1]{1,2,0:T(1,128)} %bitcast), calls=%async_computation | async-start | bytes 32768 | tf_op jit(solution)/shard_map/all_to_all | solution.py:97
  215.5 27.5 %all-to-all-start.1 = ((bf16[32,8,1024]{2,1,0:T(8,128)(2,1)}), bf16[32,8,1024]{2,1,0:T(8,128)(2,1)S(1)}, u32[]{:S(2)}, u32[]{:S(2)}) async-start(bf16[32,8,1024]{2,1,0:T(8,128)(2,1)} %fusion.13), calls=%async_computation.1 | async-start | bytes 1048576 | tf_op jit(solution)/shard_map/all_to_all | solution.py:96
  243.4 1.0 copy-start.5
  243.4 1.0 copy-start.9
  243.4 1.0 copy-start.10
  247.0 44.7 %all-to-all-start.2 = ((bf16[32,384,64]{1,2,0:T(8,128)(2,1)}), bf16[32,384,64]{1,2,0:T(8,128)(2,1)S(1)}, u32[]{:S(2)}, u32[]{:S(2)}) async-start(bf16[32,384,64]{1,2,0:T(8,128)(2,1)} %stack.3), calls=%async_computation.2 | async-start | bytes 3145728 | tf_op jit(solution)/shard_map/all_to_all | solution.py:13
  251.9 83.4 %all-gather.3.cloned.1.call-start = ((), (), s32[]{:S(2)}) async-start(), calls=%async_computation.5 | async-start | bytes 1622016 | tf_op jit(solution)/shard_map/all_gather | solution.py:120
Sparse Core Ops, SparseCore 0:
  34.3 62.1 reduce-scatter.3
  101.0 112.4 all-reduce.1
  255.8 79.4 all-gather.2
